TPU v7x, 256 devices: a whole 4x4x8 slice. The times are simulated.
256 devices in a mesh: row: 2 (over core), col: 2 (over x_lo), rhs: 64 (over z, y, x_hi).
Axes of the slice: x: 4 (x_hi: 2, x_lo: 2; x = x_hi * 2 + x_lo), y: 4, z: 8, core: 2. Of those that a mesh axis runs over, the one named last changes fastest.
Arguments:
- front: bfloat16 [4096, 4096], P(('row', 'rhs'), 'col'), as said below
- anc_weight: bfloat16 [1024, 4096], P(('row', 'rhs'), 'col'), may hold values from -0.1875 to 0.1875
- solved: bfloat16 [2048, 8192], P(('row', 'col'), 'rhs'), may hold values from -6 to 6
- owners: int32 [8], replicated, may hold values from 0 to 3, as said below
- indices: int32 [8, 128], replicated, may hold values from 0 to 511
- counts: int32 [8], replicated, may hold values from 64 to 128, as said below
- rhs_side: bfloat16 [4096, 8192], P('row', 'rhs'), may hold values from -6 to 6
Outputs:
- solution: bfloat16 [4096, 8192], P('row', 'rhs')
Inputs may be any that keep to these rules, and one draw needn't show every extreme that they name: `front`: zero above the diagonal; diagonal entries 1 or more. The 4 tiles of each aligned block of 4 tiles have 4 different owners, numbered row index times 2 plus col index. `counts`: rows at or past a tile's count are padding.
All inputs are finite; a program needn't handle non-finite values.
Results may differ from a plain program's by a relative error of at most 0.0038.
Values may be sent and summed in bfloat16 or wider, within the bound.
No kernel may reach another device: no remote copies, remote signals or barrier semaphores. Data moves between devices by JAX's collectives and lax.ppermute only.
A program may use at most 128 MiB of HBM per device.

v0:
```python
import jax
import jax.numpy as jnp
from jax import lax
from jax.sharding import PartitionSpec as P
from jax.experimental import pallas as pl
from jax.experimental.pallas import tpu as pltpu

BLOCK = 128


def split_bf16(x):
    hi = x.astype(jnp.bfloat16)
    return hi, (x - hi.astype(jnp.float32)).astype(jnp.bfloat16)


def mm3(a, b):
    a_hi, a_lo = split_bf16(a)
    b_hi, b_lo = split_bf16(b)
    eq = "bij,bjk->bik"
    out = jnp.einsum(eq, a_hi, b_hi, preferred_element_type=jnp.float32)
    out = out + jnp.einsum(eq, a_lo, b_hi, preferred_element_type=jnp.float32)
    return out + jnp.einsum(eq, a_hi, b_lo, preferred_element_type=jnp.float32)


def diag_kernel(left_hbm, right_hbm, o_ref, sems):
    nb = o_ref.shape[0]
    half = nb // 2
    copies = []
    for j in range(nb):
        src, col = (left_hbm, j) if j < half else (right_hbm, j - half)
        copies.append(
            pltpu.make_async_copy(
                src.at[pl.ds(j * BLOCK, BLOCK), pl.ds(col * BLOCK, BLOCK)], o_ref.at[j], sems.at[j]
            )
        )
    for one in copies:
        one.start()
    for one in copies:
        one.wait()


def prepare(left, right):
    n = left.shape[0]
    nb = n // BLOCK
    blocks = pl.pallas_call(
        diag_kernel,
        in_specs=[pl.BlockSpec(memory_space=pl.ANY)] * 2,
        out_specs=pl.BlockSpec(memory_space=pltpu.VMEM),
        out_shape=jax.ShapeDtypeStruct((nb, BLOCK, BLOCK), left.dtype),
        scratch_shapes=[pltpu.SemaphoreType.DMA((nb,))],
    )(left, right).astype(jnp.float32)
    eye = jnp.eye(BLOCK, dtype=jnp.float32)
    diag = jnp.sum(blocks * eye[None], axis=2)
    lower = jnp.tril(jnp.ones((BLOCK, BLOCK), jnp.bool_), -1)
    nil = jnp.where(lower[None], blocks / diag[:, :, None], 0.0)
    prod = eye[None] - nil
    power = nil
    steps = 1
    while 2 ** steps < BLOCK:
        power = mm3(power, power)
        prod = mm3(prod, eye[None] + power)
        steps += 1
    return prod, 1.0 / diag


def solve_kernel(fl_ref, fr_ref, p_ref, d_ref, r_ref, o_ref, rest_ref):
    nb = p_ref.shape[0]
    rest_ref[...] = r_ref[...]

    def body(i, carry):
        j = nb - 1 - i
        start = pl.multiple_of(j * BLOCK, BLOCK)
        r_hi, r_lo = split_bf16(rest_ref[:, pl.ds(start, BLOCK)])
        p_hi, p_lo = split_bf16(p_ref[j])
        v = jnp.dot(r_hi, p_hi, preferred_element_type=jnp.float32)
        v = v + jnp.dot(r_lo, p_hi, preferred_element_type=jnp.float32)
        v = v + jnp.dot(r_hi, p_lo, preferred_element_type=jnp.float32)
        v = v * d_ref[pl.ds(j, 1), :]
        v_hi, v_lo = split_bf16(v)
        half = rest_ref.shape[1] // 2
        for f_ref, cols in ((fl_ref, slice(0, half)), (fr_ref, slice(half, 2 * half))):
            rows = f_ref[pl.ds(start, BLOCK), :half]
            upd = jnp.dot(v_hi, rows, preferred_element_type=jnp.float32)
            upd = upd + jnp.dot(v_lo, rows, preferred_element_type=jnp.float32)
            rest_ref[:, cols] = rest_ref[:, cols] - upd
        o_ref[:, pl.ds(start, BLOCK)] = v.astype(o_ref.dtype)
        return carry

    lax.fori_loop(0, nb, body, 0)


def kernel_solve(left, right, prod, inv_diag, rhs):
    n = rhs.shape[0]
    cols = rhs.shape[1]
    vmem = pl.BlockSpec(memory_space=pltpu.VMEM)
    out_t = pl.pallas_call(
        solve_kernel,
        out_shape=jax.ShapeDtypeStruct((cols, n), jnp.bfloat16),
        in_specs=[vmem, vmem, vmem, vmem, vmem],
        out_specs=vmem,
        scratch_shapes=[pltpu.VMEM((cols, n), jnp.float32)],
        compiler_params=pltpu.CompilerParams(vmem_limit_bytes=48 * 1024 * 1024),
    )(left, right, prod, inv_diag, rhs.T)
    return out_t.T


def chunked_permute(x, axis, perm, parts=4):
    pieces = jnp.split(x, parts, axis=0)
    return jnp.concatenate([lax.ppermute(p, axis, perm) for p in pieces], axis=0)


def ancestor_values(solved, owners, indices, counts):
    row_count = lax.axis_size("row")
    col_count = lax.axis_size("col")
    tiles_block = row_count * col_count
    row_index = lax.axis_index("row")
    col_index = lax.axis_index("col")
    tile_rows = indices.shape[1]
    columns = solved.shape[1]
    self_id = row_index * col_count + col_index
    owner_grid = owners.reshape(row_count, tiles_block)
    mine = (owner_grid == self_id).astype(jnp.int32)
    position = jnp.sum(mine * jnp.arange(tiles_block, dtype=jnp.int32)[None, :], axis=1)
    tile_ids = jnp.arange(row_count, dtype=jnp.int32) * tiles_block + position
    local_rows = indices[tile_ids]
    live_rows = jnp.arange(tile_rows, dtype=jnp.int32)[None, :] < counts[tile_ids][:, None]
    picked = solved[local_rows.reshape(-1)].reshape(row_count, tile_rows, columns)
    picked = jnp.where(live_rows[:, :, None], picked, jnp.zeros_like(picked))
    block_owners = lax.dynamic_slice_in_dim(owners, row_index * tiles_block, tiles_block)
    outgoing = jnp.broadcast_to(picked[:, None], (row_count, col_count, tile_rows, columns))
    outgoing = outgoing.reshape(row_count * col_count * tile_rows, columns)
    received = lax.all_to_all(outgoing, ("row", "col"), split_axis=0, concat_axis=0, tiled=True)
    slot_rows = received.reshape(tiles_block, tile_rows, columns)
    anc_values = slot_rows[block_owners].reshape(tiles_block * tile_rows, columns)
    return anc_values


def device_body(front, anc_weight, solved, owners, indices, counts, rhs_side):
    row_index = lax.axis_index("row")
    col_index = lax.axis_index("col")
    shard_rows, width = front.shape
    half = width // 2
    w_rows = anc_weight.shape[0]
    fold = shard_rows // w_rows
    partner = lax.ppermute(front, "row", [(0, 1), (1, 0)])
    first_owner = row_index == col_index
    half_one = jnp.where(first_owner, front[:, half:], partner[:, :half])
    both = jnp.concatenate([half_one, anc_weight.reshape(shard_rows, width // fold)], axis=1)
    both = lax.all_gather(both, "xh", axis=0, tiled=True)
    both = lax.all_gather(both, "y", axis=0, tiled=True)
    anc_values = ancestor_values(solved, owners, indices, counts)
    both = lax.all_gather(both, "z", axis=0, tiled=True)
    weight_tile = both[:, half:].reshape(-1, w_rows, fold, width // fold).reshape(-1, width)
    crit_left = lax.ppermute(both[:, :half], ("row", "col"), [(2, 0), (1, 3)])
    crit_right = both
    anc_total = lax.dot_general(
        weight_tile, anc_values, (((0,), (0,)), ((), ())), preferred_element_type=jnp.float32
    )
    prod, inv_diag = prepare(crit_left, crit_right)

    second_owner = row_index == 1 - col_index
    half_two = jnp.where(second_owner, front[:, half:], partner[:, :half])
    half_two, _ = lax.optimization_barrier((half_two, both))
    half_two = lax.all_gather(half_two, ("z", "y", "xh"), axis=0, tiled=True)
    prod_left = lax.ppermute(half_two, ("row", "col"), [(0, 2), (3, 1)])
    prod_right = half_two

    rhs_values = rhs_side.astype(jnp.float32)
    down = [(1, 0)]
    left = [(1, 0)]
    right = [(0, 1)]

    own_one = anc_total.astype(jnp.bfloat16)
    other_one = lax.ppermute(own_one, "row", [(0, 1)])
    reduced_one = rhs_values - own_one.astype(jnp.float32) - other_one.astype(jnp.float32)
    sol_one = kernel_solve(crit_left, crit_right, prod, inv_diag, reduced_one)
    got_one = chunked_permute(sol_one, "col", left)
    sol_one = jnp.where(col_index == 1, sol_one, got_one)

    dims = (((0,), (0,)), ((), ()))
    front_term = jnp.concatenate(
        [
            lax.dot_general(prod_left, sol_one, dims, preferred_element_type=jnp.float32),
            lax.dot_general(prod_right, sol_one, dims, preferred_element_type=jnp.float32),
        ],
        axis=0,
    )
    own_zero = (anc_total + front_term).astype(jnp.bfloat16)
    own_zero = jnp.where(row_index == 0, anc_total.astype(jnp.bfloat16), own_zero)
    other_zero = lax.ppermute(own_zero, "row", down)
    reduced_zero = rhs_values - own_zero.astype(jnp.float32) - other_zero.astype(jnp.float32)
    sol_zero = kernel_solve(crit_left, crit_right, prod, inv_diag, reduced_zero)
    got_zero = chunked_permute(sol_zero, "col", right)
    sol_zero = jnp.where(col_index == 0, sol_zero, got_zero)
    return jnp.where(row_index == 1, sol_one, sol_zero)


def solution(mesh):
    dims = dict(mesh.shape)
    rhs_split = (dims["rhs"] // 8, 4, 2)
    sub = jax.sharding.Mesh(
        mesh.devices.reshape(dims["row"], dims["col"], *rhs_split), ("row", "col", "z", "y", "xh")
    )
    rhs = ("z", "y", "xh")
    placed = (
        P(("row",) + rhs, "col"),
        P(("row",) + rhs, "col"),
        P(("row", "col"), rhs),
        P(),
        P(),
        P(),
        P("row", rhs),
    )
    return jax.shard_map(
        device_body, mesh=sub, in_specs=placed, out_specs=P("row", rhs), check_vma=False
    )
```

profile of v0, /device:TPU:6, one launch (start us, length us, event | category | flops | bytes accessed | tf_op | source)
XLA Modules:
  0.0 344.7 jit_solution(15714369096752249269)
XLA Ops:
  6.5 0.8 reshape.122
  7.4 0.7 collective-permute-done
  8.1 1.5 broadcast_select_fusion
  9.6 7.0 %all_gather.12 = bf16[64,1536]{1,0:T(8,128)(2,1)S(1)} all-gather(bf16[32,1536]{1,0:T(8,128)(2,1)S(1)} %pad_maximum_fusion), channel_id=1, replica_groups=mesh['row'=2,'col'=2,'z'=8,'y'=4,'xh'=2] {'xh'}, dimensions={0}, use_global_device_ids=true | all-gather | bytes 294912 | tf_op jit(solution)/shard_map/all_gather | solution.py:149
  16.6 14.6 %all_gather.13 = bf16[256,1536]{1,0:T(8,128)(2,1)} all-gather(bf16[64,1536]{1,0:T(8,128)(2,1)S(1)} %all_gather.12), channel_id=1, replica_groups=mesh['row'=2,'col'=2,'z'=8,'y'=4,'xh'=2] {'y'}, dimensions={0}, use_global_device_ids=true | all-gather | bytes 983040 | tf_op jit(solution)/shard_map/all_gather | solution.py:150
  31.2 77.8 %all-gather.3.cloned.1.call-done.right_hbm.fr_ref = bf16[2048,1536]{1,0:T(8,128)(2,1)} async-done(((bf16[256,1536]{1,0:T(8,128)(2,1)}), bf16[2048,1536]{1,0:T(8,128)(2,1)}) %all-gather.3.cloned.1.call-update) | async-done | bytes 6291472 | tf_op jit(solution)/shard_map/all_gather | solution.py:152
  109.0 4.6 %slice.27 = bf16[2048,1024]{1,0:T(8,128)(2,1)} slice(bf16[2048,1536]{1,0:T(8,128)(2,1)} %all-gather.3.cloned.1.call-done.right_hbm.fr_ref), slice={[0:2048], [0:1024]} | slice | bytes 8388608 | tf_op jit(solution)/shard_map/slice | solution.py:154
  113.6 3.8 %collective-permute-start.1 = (bf16[2048,1024]{1,0:T(8,128)(2,1)}, bf16[2048,1024]{1,0:T(8,128)(2,1)}, u32[]{:S(2)}, u32[]{:S(2)}) collective-permute-start(bf16[2048,1024]{1,0:T(8,128)(2,1)} %slice.27), channel_id=1, source_target_pairs={{128,0},{64,192},{129,1},{65,193},{130,2},{66,194},{131,3},{67,195... | collective-permute-start | bytes 12582920 | tf_op jit(solution)/shard_map/ppermute | solution.py:154
  118.9 0.9 gather_fusion.2
  119.9 0.7 broadcast_in_dim.28
  120.6 3.3 all-to-all-start
  124.0 3.3 all-to-all-done
  127.9 2.6 reshape_reshape.3
  130.5 3.1 fusion.74
  133.6 1.6 collective-permute-start.2
  135.6 0.9 collective-permute-done.2
  136.8 1.9 shard_map.73
  138.7 1.4 fusion.1
  140.2 2.0 fusion.18
  142.2 0.9 convolution_add_fusion.23
  143.1 0.9 convolution_add_fusion.22
  147.6 1.3 fusion.38
  153.3 1.4 convolution_add_fusion.9
  154.6 106.0 %all-gather.5.cloned.1.call-done = bf16[2048,1024]{1,0:T(8,128)(2,1)} async-done(((bf16[32,1024]{1,0:T(8,128)(2,1)}), bf16[2048,1024]{1,0:T(8,128)(2,1)}) %all-gather.5.cloned.1.call-update) | async-done | bytes 4194320 | tf_op jit(solution)/shard_map/all_gather | solution.py:164
  260.6 1.6 collective-permute-start.7
  262.2 1.9 convolution_add_fusion.8
  266.6 13.9 %shard_map.74 = bf16[128,2048]{1,0:T(8,128)(2,1)S(1)} custom-call(bf16[2048,1024]{1,0:T(8,128)(2,1)} %collective-permute-done.1.left_hbm.fl_ref, bf16[2048,1536]{1,0:T(8,128)(2,1)} %all-gather.3.cloned.1.call-done.right_hbm.fr_ref, f32[16,128,128]{2,1,0:T(8,128)S(1)} %convolution_add_fusion.p_ref, f32[16,128]{1,0:T(8,128)S(1)} %broadcast_divide_fusion.d_ref, ...), custom_call_target="tpu_custom_call" | custom-call | tf_op jit(solution)/shard_map/pallas_call | solution.py:96
  280.5 3.6 %collective-permute-start.3 = (bf16[512,128]{0,1:T(8,128)(2,1)S(1)}, bf16[512,128]{0,1:T(8,128)(2,1)S(1)}, u32[]{:S(2)}, u32[]{:S(2)}) collective-permute-start(bf16[512,128]{0,1:T(8,128)(2,1)S(1)} %get-tuple-element.11), channel_id=1, source_target_pairs={{64,0},{65,1},{66,2},{67,3},{68,4},{69,5},{70,6},{71,7},{72,8},{73... | collective-permute-start | bytes 393224 | tf_op jit(solution)/shard_map/ppermute | solution.py:109
  284.1 1.3 collective-permute-start.4
  285.4 1.3 collective-permute-start.5
  286.8 1.3 collective-permute-start.6
  288.1 2.7 collective-permute-done.4
  290.8 2.8 collective-permute-done.5
  293.6 2.7 collective-permute-done.6
  296.5 3.0 fusion.76
  299.5 3.0 fusion.75
  302.7 1.3 collective-permute-start.8
  304.0 2.5 collective-permute-done.8
  306.7 13.9 %shard_map.75 = bf16[128,2048]{1,0:T(8,128)(2,1)S(1)} custom-call(bf16[2048,1024]{1,0:T(8,128)(2,1)} %collective-permute-done.1.left_hbm.fl_ref, bf16[2048,1536]{1,0:T(8,128)(2,1)} %all-gather.3.cloned.1.call-done.right_hbm.fr_ref, f32[16,128,128]{2,1,0:T(8,128)S(1)} %convolution_add_fusion.p_ref, f32[16,128]{1,0:T(8,128)S(1)} %broadcast_divide_fusion.d_ref, ...), custom_call_target="tpu_custom_call" | custom-call | tf_op jit(solution)/shard_map/pallas_call | solution.py:96
  320.7 1.3 collective-permute-start.10
  322.0 1.3 collective-permute-start.11
  323.3 1.3 collective-permute-start.12
  324.6 1.3 collective-permute-start.9
  325.9 3.1 collective-permute-done.10
  328.9 2.8 collective-permute-done.11
  331.7 2.8 collective-permute-done.12
  334.6 2.1 collective-permute-done.9
  336.9 1.0 copy.19
  (94 shorter events, 14.1 us)
Async XLA Ops:
  6.5 112.3 %copy-start = (bf16[512,128]{1,0:T(8,128)(2,1)S(1)}, bf16[512,128]{1,0:T(8,128)(2,1)}, u32[]{:S(2)}) copy-start(bf16[512,128]{1,0:T(8,128)(2,1)} %param.9) | copy-start | bytes 393220
  6.5 102.5 %all-gather.3.cloned.1.call-start = ((), (), s32[]{:S(2)}) async-start(), calls=%async_computation.1 | async-start | bytes 7077888 | tf_op jit(solution)/shard_map/all_gather | solution.py:152
  6.5 1.6 collective-permute-start
  31.2 86.2 %copy-start.13 = (s32[8]{0:T(128)S(1)}, s32[8]{0:T(128)}, u32[]{:S(2)}) copy-start(s32[8]{0:T(128)} %param.10) | copy-start | bytes 100
  31.2 86.4 %copy-start.12 = (s32[8,128]{1,0:T(8,128)S(1)}, s32[8,128]{1,0:T(8,128)}, u32[]{:S(2)}) copy-start(s32[8,128]{1,0:T(8,128)} %param.11) | copy-start | bytes 12292
  31.2 87.0 %copy-start.2 = (s32[8]{0:T(128)S(1)}, s32[8]{0:T(128)}, u32[]{:S(2)}) copy-start(s32[8]{0:T(128)} %param.12) | copy-start | bytes 100
  113.6 14.3 %slice-start = ((bf16[2048,1536]{1,0:T(8,128)(2,1)}), bf16[2048,512]{1,0:T(8,128)(2,1)S(1)}, s32[]{:S(2)}) async-start(bf16[2048,1536]{1,0:T(8,128)(2,1)} %all-gather.3.cloned.1.call-done.right_hbm.fr_ref), calls=%async_computation.3 | async-start | bytes 4194304 | tf_op jit(solution)/shard_map/slice | solution.py:153
  113.6 23.1 %collective-permute-start.1 = (bf16[2048,1024]{1,0:T(8,128)(2,1)}, bf16[2048,1024]{1,0:T(8,128)(2,1)}, u32[]{:S(2)}, u32[]{:S(2)}) collective-permute-start(bf16[2048,1024]{1,0:T(8,128)(2,1)} %slice.27), channel_id=1, source_target_pairs={{128,0},{64,192},{129,1},{65,193},{130,2},{66,194},{131,3},{67,195... | collective-permute-start | bytes 12582920 | tf_op jit(solution)/shard_map/ppermute | solution.py:154
  120.6 6.8 %all-to-all-start = ((bf16[4,128,128]{2,1,0:T(8,128)(2,1)}), bf16[4,128,128]{2,1,0:T(8,128)(2,1)S(1)}, u32[]{:S(2)}, u32[]{:S(2)}) async-start(bf16[4,128,128]{2,1,0:T(8,128)(2,1)} %bitcast.5), calls=%async_computation | async-start | bytes 262144 | tf_op jit(solution)/shard_map/all_to_all | solution.py:132
  123.9 136.7 %all-gather.5.cloned.1.call-start = ((), (), s32[]{:S(2)}) async-start(), calls=%async_computation.2 | async-start | bytes 4259840 | tf_op jit(solution)/shard_map/all_gather | solution.py:164
  130.5 4.7 %copy-start.11 = (bf16[2048,128]{1,0:T(8,128)(2,1)S(1)}, bf16[2048,128]{1,0:T(8,128)(2,1)}, u32[]{:S(2)}) copy-start(bf16[2048,128]{1,0:T(8,128)(2,1)} %param.13) | copy-start | bytes 1572868
  133.6 5.1 %copy-start.5 = (bf16[2048,128]{0,1:T(8,128)(2,1)}, bf16[2048,128]{0,1:T(8,128)(2,1)S(1)}, u32[]{:S(2)}) copy-start(bf16[2048,128]{0,1:T(8,128)(2,1)S(1)} %get-tuple-element.17) | copy-start | bytes 1572868
  133.6 2.9 collective-permute-start.2
  135.4 3.3 copy-start.7
  138.7 3.5 %copy-start.10 = (bf16[16,128,128]{2,1,0:T(8,128)(2,1)S(1)}, bf16[16,128,128]{2,1,0:T(8,128)(2,1)}, u32[]{:S(2)}) copy-start(bf16[16,128,128]{2,1,0:T(8,128)(2,1)} %shard_map.73) | copy-start | bytes 1572868
  152.2 1.0 copy-start.3
  260.6 3.9 %copy-start.9 = (f32[16,128,128]{2,1,0:T(8,128)S(1)}, f32[16,128,128]{2,1,0:T(8,128)}, u32[]{:S(2)}) copy-start(f32[16,128,128]{2,1,0:T(8,128)} %fusion.38) | copy-start | bytes 3145732
  260.6 38.9 %collective-permute-start.7 = (bf16[2048,1024]{1,0:T(8,128)(2,1)}, bf16[2048,1024]{1,0:T(8,128)(2,1)}, u32[]{:S(2)}, u32[]{:S(2)}) collective-permute-start(bf16[2048,1024]{1,0:T(8,128)(2,1)} %all-gather.5.cloned.1.call-done), channel_id=1, source_target_pairs={{0,128},{192,64},{1,129},{193,65},{2,130},{194,66},{3,131},{195,67... | collective-permute-start | bytes 12582920 | tf_op jit(solution)/shard_map/ppermute | solution.py:165
  280.5 7.5 %collective-permute-start.3 = (bf16[512,128]{0,1:T(8,128)(2,1)S(1)}, bf16[512,128]{0,1:T(8,128)(2,1)S(1)}, u32[]{:S(2)}, u32[]{:S(2)}) collective-permute-start(bf16[512,128]{0,1:T(8,128)(2,1)S(1)} %get-tuple-element.11), channel_id=1, source_target_pairs={{64,0},{65,1},{66,2},{67,3},{68,4},{69,5},{70,6},{71,7},{72,8},{73... | collective-permute-start | bytes 393224 | tf_op jit(solution)/shard_map/ppermute | solution.py:109
  284.1 6.7 %collective-permute-start.4 = (bf16[512,128]{0,1:T(8,128)(2,1)S(1)}, bf16[512,128]{0,1:T(8,128)(2,1)S(1)}, u32[]{:S(2)}, u32[]{:S(2)}) collective-permute-start(bf16[512,128]{0,1:T(8,128)(2,1)S(1)} %get-tuple-element.14), channel_id=1, source_target_pairs={{64,0},{65,1},{66,2},{67,3},{68,4},{69,5},{70,6},{71,7},{72,8},{73... | collective-permute-start | bytes 393224 | tf_op jit(solution)/shard_map/ppermute | solution.py:109
  285.4 8.2 %collective-permute-start.5 = (bf16[512,128]{0,1:T(8,128)(2,1)S(1)}, bf16[512,128]{0,1:T(8,128)(2,1)S(1)}, u32[]{:S(2)}, u32[]{:S(2)}) collective-permute-start(bf16[512,128]{0,1:T(8,128)(2,1)S(1)} %get-tuple-element.13), channel_id=1, source_target_pairs={{64,0},{65,1},{66,2},{67,3},{68,4},{69,5},{70,6},{71,7},{72,8},{73... | collective-permute-start | bytes 393224 | tf_op jit(solution)/shard_map/ppermute | solution.py:109
  286.8 9.6 %collective-permute-start.6 = (bf16[512,128]{0,1:T(8,128)(2,1)S(1)}, bf16[512,128]{0,1:T(8,128)(2,1)S(1)}, u32[]{:S(2)}, u32[]{:S(2)}) collective-permute-start(bf16[512,128]{0,1:T(8,128)(2,1)S(1)} %get-tuple-element.12), channel_id=1, source_target_pairs={{64,0},{65,1},{66,2},{67,3},{68,4},{69,5},{70,6},{71,7},{72,8},{73... | collective-permute-start | bytes 393224 | tf_op jit(solution)/shard_map/ppermute | solution.py:109
  296.5 6.0 %copy-start.4 = (f32[2048,128]{0,1:T(8,128)S(1)}, f32[2048,128]{0,1:T(8,128)}, u32[]{:S(2)}) copy-start(f32[2048,128]{0,1:T(8,128)} %get-tuple-element.18) | copy-start | bytes 3145732
  296.5 6.0 %copy-start.6 = (bf16[2048,128]{0,1:T(8,128)(2,1)S(1)}, bf16[2048,128]{0,1:T(8,128)(2,1)}, u32[]{:S(2)}) copy-start(bf16[2048,128]{0,1:T(8,128)(2,1)} %copy-done.5) | copy-start | bytes 1572868
  299.5 7.0 %copy-start.8 = (bf16[2048,128]{0,1:T(8,128)(2,1)S(1)}, bf16[2048,128]{0,1:T(8,128)(2,1)}, u32[]{:S(2)}) copy-start(bf16[2048,128]{0,1:T(8,128)(2,1)} %copy-done.7) | copy-start | bytes 1572868
  302.7 3.8 %collective-permute-start.8 = (bf16[2048,128]{0,1:T(8,128)(2,1)S(1)}, bf16[2048,128]{0,1:T(8,128)(2,1)S(1)}, u32[]{:S(2)}, u32[]{:S(2)}) collective-permute-start(bf16[2048,128]{0,1:T(8,128)(2,1)S(1)} %fusion.8), channel_id=1, source_target_pairs={{128,0},{129,1},{130,2},{131,3},{132,4},{133,5},{134,6},{135,7},{1... | collective-permute-start | bytes 1572872 | tf_op jit(solution)/shard_map/ppermute | solution.py:190
  306.7 31.1 %copy-start.1 = (bf16[512,128]{1,0:T(8,128)(2,1)S(1)}, bf16[512,128]{1,0:T(8,128)(2,1)}, u32[]{:S(2)}) copy-start(bf16[512,128]{1,0:T(8,128)(2,1)} %param.9) | copy-start | bytes 393220
  320.7 8.3 %collective-permute-start.10 = (bf16[512,128]{0,1:T(8,128)(2,1)S(1)}, bf16[512,128]{0,1:T(8,128)(2,1)S(1)}, u32[]{:S(2)}, u32[]{:S(2)}) collective-permute-start(bf16[512,128]{0,1:T(8,128)(2,1)S(1)} %get-tuple-element.10), channel_id=1, source_target_pairs={{0,64},{1,65},{2,66},{3,67},{4,68},{5,69},{6,70},{7,71},{8,72},{9,... | collective-permute-start | bytes 393224 | tf_op jit(solution)/shard_map/ppermute | solution.py:109
  322.0 9.8 %collective-permute-start.11 = (bf16[512,128]{0,1:T(8,128)(2,1)S(1)}, bf16[512,128]{0,1:T(8,128)(2,1)S(1)}, u32[]{:S(2)}, u32[]{:S(2)}) collective-permute-start(bf16[512,128]{0,1:T(8,128)(2,1)S(1)} %get-tuple-element.9), channel_id=1, source_target_pairs={{0,64},{1,65},{2,66},{3,67},{4,68},{5,69},{6,70},{7,71},{8,72},{9,... | collective-permute-start | bytes 393224 | tf_op jit(solution)/shard_map/ppermute | solution.py:109
  323.3 11.3 %collective-permute-start.12 = (bf16[512,128]{0,1:T(8,128)(2,1)S(1)}, bf16[512,128]{0,1:T(8,128)(2,1)S(1)}, u32[]{:S(2)}, u32[]{:S(2)}) collective-permute-start(bf16[512,128]{0,1:T(8,128)(2,1)S(1)} %get-tuple-element.8), channel_id=1, source_target_pairs={{0,64},{1,65},{2,66},{3,67},{4,68},{5,69},{6,70},{7,71},{8,72},{9,... | collective-permute-start | bytes 393224 | tf_op jit(solution)/shard_map/ppermute | solution.py:109
  324.6 12.1 %collective-permute-start.9 = (bf16[512,128]{0,1:T(8,128)(2,1)S(1)}, bf16[512,128]{0,1:T(8,128)(2,1)S(1)}, u32[]{:S(2)}, u32[]{:S(2)}) collective-permute-start(bf16[512,128]{0,1:T(8,128)(2,1)S(1)} %get-tuple-element.7), channel_id=1, source_target_pairs={{0,64},{1,65},{2,66},{3,67},{4,68},{5,69},{6,70},{7,71},{8,72},{9,... | collective-permute-start | bytes 393224 | tf_op jit(solution)/shard_map/ppermute | solution.py:109
Sparse Core Ops, SparseCore 0:
  31.3 77.6 all-gather.2
  135.7 124.8 all-gather.4
where the time goes:
time: 346 us; the launch traced here: 345 us
  waiting for transfers between devices  210 us (61%)
  Pallas kernels  29.7 us (9%)
  matrix products  27 us (8%)
  starting transfers between devices  24.3 us (7%)
  blocking collectives  21.6 us (6%)
  between operations  14 us (4%)
  local copies, waits for them, and re-layouts  13.4 us (4%)
  other arithmetic  4.44 us (1%)
    all_gather x1, waiting for transfers between devices, device_body(): half_two = lax.all_gather(half_two, ('z', 'y', 'xh'), axis=0, tiled=True)  106 us
    all_gather x1, waiting for transfers between devices, device_body(): both = lax.all_gather(both, 'z', axis=0, tiled=True)  77.8 us
    pallas_call x2, Pallas kernels, kernel_solve(): pl.pallas_call(solve_kernel, out_shape=jax.ShapeDtypeStruct((cols, n), jn...  27.7 us
    ppermute x8, waiting for transfers between devices, chunked_permute(): lax.ppermute(p, axis, perm)  19 us
    all_gather x1, blocking collectives, device_body(): both = lax.all_gather(both, 'y', axis=0, tiled=True)  14.6 us
    ppermute x8, starting transfers between devices, chunked_permute(): lax.ppermute(p, axis, perm)  12.7 us
    all_gather x1, blocking collectives, device_body(): both = lax.all_gather(both, 'xh', axis=0, tiled=True)  7.02 us
  transfers between devices with their start and end apart: 16, of which 13 were waited for; matrix products, arithmetic and copies ran while one was open for 10% of the time, Pallas kernels for 5%

commit v1 on v0

--- a/solution.py
+++ b/solution.py
@@ -151,7 +151,7 @@
     anc_values = ancestor_values(solved, owners, indices, counts)
     both = lax.all_gather(both, "z", axis=0, tiled=True)
     weight_tile = both[:, half:].reshape(-1, w_rows, fold, width // fold).reshape(-1, width)
-    crit_left = lax.ppermute(both[:, :half], ("row", "col"), [(2, 0), (1, 3)])
+    crit_left = lax.ppermute(both, ("row", "col"), [(2, 0), (1, 3)])
     crit_right = both
     anc_total = lax.dot_general(
         weight_tile, anc_values, (((0,), (0,)), ((), ())), preferred_element_type=jnp.float32
@@ -160,10 +160,10 @@
 
     second_owner = row_index == 1 - col_index
     half_two = jnp.where(second_owner, front[:, half:], partner[:, :half])
+    half_two = lax.all_gather(half_two, "xh", axis=0, tiled=True)
+    half_two = lax.all_gather(half_two, "y", axis=0, tiled=True)
     half_two, _ = lax.optimization_barrier((half_two, both))
-    half_two = lax.all_gather(half_two, ("z", "y", "xh"), axis=0, tiled=True)
-    prod_left = lax.ppermute(half_two, ("row", "col"), [(0, 2), (3, 1)])
-    prod_right = half_two
+    half_two = lax.all_gather(half_two, "z", axis=0, tiled=True)
 
     rhs_values = rhs_side.astype(jnp.float32)
     down = [(1, 0)]
@@ -175,7 +175,10 @@
     reduced_one = rhs_values - own_one.astype(jnp.float32) - other_one.astype(jnp.float32)
     sol_one = kernel_solve(crit_left, crit_right, prod, inv_diag, reduced_one)
     got_one = chunked_permute(sol_one, "col", left)
+    half_two, got_one = lax.optimization_barrier((half_two, got_one))
     sol_one = jnp.where(col_index == 1, sol_one, got_one)
+    prod_left = lax.ppermute(half_two, ("row", "col"), [(0, 2), (3, 1)])
+    prod_right = half_two
 
     dims = (((0,), (0,)), ((), ()))
     front_term = jnp.concatenate(

time: 346 us -> 264 us (0.76)
  waiting for transfers between devices: 210 us -> 112 us
  blocking collectives: 21.6 us -> 42.7 us
  matrix products: 27 us -> 21.9 us
    all_gather x1, waiting for transfers between devices: 106 us -> 9.78 us  [device_body(): half_two = lax.all_gather(half_two, 'z', axis=0, tiled=True)]
    all_gather x0 -> x2, blocking collectives: none -> 21.1 us  [the longest x1 14.7 us: device_body(): half_two = lax.all_gather(half_two, 'y', axis=0, tiled=True)]
    ppermute x8, waiting for transfers between devices: 19 us -> 13.4 us  [chunked_permute(): lax.ppermute(p, axis, perm)]
    ppermute x1, waiting for transfers between devices: 0.01 us -> 4.98 us  [device_body(): prod_left = lax.ppermute(half_two, ('row', 'col'), [(0, 2), (3, 1)])]
    slice x1 -> x0, local copies, waits for them, and re-layouts: 4.59 us -> none  [device_body(): crit_left = lax.ppermute(both[:, :half], ('row', 'col'), [(2, 0), (1, 3)])]
  transfers between devices with their start and end apart: 16 -> 16, of which waited for: 13 -> 12; matrix products, arithmetic and copies ran while one was open for 10% -> 13% of each run, Pallas kernels for 5% -> 6%
where the time goes in v1:
time: 264 us; the launch traced here: 263 us
  waiting for transfers between devices  112 us (42%)
  blocking collectives  42.7 us (16%)
  Pallas kernels  30.9 us (12%)
  starting transfers between devices  23.7 us (9%)
  matrix products  21.9 us (8%)
  between operations  14.1 us (5%)
  local copies, waits for them, and re-layouts  13 us (5%)
  other arithmetic  4.41 us (2%)
    all_gather x1, waiting for transfers between devices, device_body(): both = lax.all_gather(both, 'z', axis=0, tiled=True)  77.8 us
    pallas_call x2, Pallas kernels, kernel_solve(): pl.pallas_call(solve_kernel, out_shape=jax.ShapeDtypeStruct((cols, n), jn...  28.9 us
    all_gather x1, blocking collectives, device_body(): half_two = lax.all_gather(half_two, 'y', axis=0, tiled=True)  14.7 us
    all_gather x1, blocking collectives, device_body(): both = lax.all_gather(both, 'y', axis=0, tiled=True)  14.6 us
    ppermute x8, waiting for transfers between devices, chunked_permute(): lax.ppermute(p, axis, perm)  13.4 us
    ppermute x8, starting transfers between devices, chunked_permute(): lax.ppermute(p, axis, perm)  12.1 us
    all_gather x1, waiting for transfers between devices, device_body(): half_two = lax.all_gather(half_two, 'z', axis=0, tiled=True)  9.78 us
    all_gather x1, blocking collectives, device_body(): both = lax.all_gather(both, 'xh', axis=0, tiled=True)  7.02 us
  transfers between devices with their start and end apart: 16, of which 12 were waited for; matrix products, arithmetic and copies ran while one was open for 13% of the time, Pallas kernels for 6%

profile of v1, /device:TPU:6, one launch (start us, length us, event | category | flops | bytes accessed | tf_op | source)
XLA Modules:
  0.0 263.0 jit_solution(8555017582572866138)
XLA Ops:
  6.7 0.9 reshape.122
  7.5 0.7 collective-permute-done
  8.2 0.9 broadcast_select_fusion.3
  9.1 7.0 %all_gather.18 = bf16[64,1536]{1,0:T(8,128)(2,1)S(1)} all-gather(bf16[32,1536]{1,0:T(8,128)(2,1)S(1)} %pad_maximum_fusion.1), channel_id=1, replica_groups=mesh['row'=2,'col'=2,'z'=8,'y'=4,'xh'=2] {'xh'}, dimensions={0}, use_global_device_ids=true | all-gather | bytes 294912 | tf_op jit(solution)/shard_map/all_gather | solution.py:149
  16.1 14.6 %all_gather.19 = bf16[256,1536]{1,0:T(8,128)(2,1)} all-gather(bf16[64,1536]{1,0:T(8,128)(2,1)S(1)} %all_gather.18), channel_id=1, replica_groups=mesh['row'=2,'col'=2,'z'=8,'y'=4,'xh'=2] {'y'}, dimensions={0}, use_global_device_ids=true | all-gather | bytes 983040 | tf_op jit(solution)/shard_map/all_gather | solution.py:150
  30.7 77.8 %all-gather.3.cloned.1.call-done.right_hbm.fr_ref = bf16[2048,1536]{1,0:T(8,128)(2,1)} async-done(((bf16[256,1536]{1,0:T(8,128)(2,1)}), bf16[2048,1536]{1,0:T(8,128)(2,1)}) %all-gather.3.cloned.1.call-update) | async-done | bytes 6291472 | tf_op jit(solution)/shard_map/all_gather | solution.py:152
  108.5 4.2 %collective-permute-start.1 = (bf16[2048,1536]{1,0:T(8,128)(2,1)}, bf16[2048,1536]{1,0:T(8,128)(2,1)}, u32[]{:S(2)}, u32[]{:S(2)}) collective-permute-start(bf16[2048,1536]{1,0:T(8,128)(2,1)} %all-gather.3.cloned.1.call-done.right_hbm.fr_ref), channel_id=1, source_target_pairs={{128,0},{64,192},{129,1},{65,193},{130,2},{66,194},{131,3},{67,195... | collective-permute-start | bytes 18874376 | tf_op jit(solution)/shard_map/ppermute | solution.py:154
  113.5 1.2 gather_fusion.1
  114.8 1.3 gather_fusion
  116.1 0.9 gather_fusion.2
  117.2 0.7 broadcast_in_dim.28
  117.8 3.3 %all-to-all-start = ((bf16[4,128,128]{2,1,0:T(8,128)(2,1)}), bf16[4,128,128]{2,1,0:T(8,128)(2,1)S(1)}, u32[]{:S(2)}, u32[]{:S(2)}) async-start(bf16[4,128,128]{2,1,0:T(8,128)(2,1)} %bitcast.5), calls=%async_computation | async-start | bytes 262144 | tf_op jit(solution)/shard_map/all_to_all | solution.py:132
  121.5 3.0 %all-to-all-done = bf16[4,128,128]{2,1,0:T(8,128)(2,1)S(1)} async-done(((bf16[4,128,128]{2,1,0:T(8,128)(2,1)}), bf16[4,128,128]{2,1,0:T(8,128)(2,1)S(1)}, u32[]{:S(2)}, u32[]{:S(2)}) %all-to-all-start) | async-done | bytes 131104 | tf_op jit(solution)/shard_map/all_to_all | solution.py:132
  125.2 3.0 %slice.23 = bf16[2048,512]{1,0:T(8,128)(2,1)} slice(bf16[2048,1536]{1,0:T(8,128)(2,1)} %all-gather.3.cloned.1.call-done.right_hbm.fr_ref), slice={[0:2048], [1024:1536]} | slice | bytes 4194304 | tf_op jit(solution)/shard_map/slice | solution.py:153
  128.2 3.1 %reshape_reshape.3 = bf16[512,2048]{1,0:T(8,128)(2,1)S(1)} reshape(bf16[2048,512]{1,0:T(8,128)(2,1)} %slice.23) | data formatting | bytes 4194304 | tf_op jit(solution)/shard_map/reshape;reshape | solution.py:153
  131.3 1.5 fusion.74
  132.8 1.4 collective-permute-start.2
  134.3 6.4 %all_gather.21 = bf16[64,1024]{1,0:T(8,128)(2,1)S(1)} all-gather(bf16[32,1024]{1,0:T(8,128)(2,1)S(1)} %get-tuple-element.20), channel_id=1, replica_groups=mesh['row'=2,'col'=2,'z'=8,'y'=4,'xh'=2] {'xh'}, dimensions={0}, use_global_device_ids=true | all-gather | bytes 196608 | tf_op jit(solution)/shard_map/all_gather | solution.py:163
  140.7 14.7 %all_gather.22 = bf16[256,1024]{1,0:T(8,128)(2,1)} all-gather(bf16[64,1024]{1,0:T(8,128)(2,1)S(1)} %all_gather.21), channel_id=1, replica_groups=mesh['row'=2,'col'=2,'z'=8,'y'=4,'xh'=2] {'y'}, dimensions={0}, use_global_device_ids=true | all-gather | bytes 655360 | tf_op jit(solution)/shard_map/all_gather | solution.py:164
  155.7 1.9 shard_map.73
  157.7 1.4 fusion.1
  159.1 2.0 fusion.18
  161.1 0.9 convolution_add_fusion.23
  162.0 0.9 convolution_add_fusion.22
  173.8 14.5 %shard_map.74 = bf16[128,2048]{1,0:T(8,128)(2,1)S(1)} custom-call(bf16[2048,1536]{1,0:T(8,128)(2,1)} %collective-permute-done.1.left_hbm.fl_ref, bf16[2048,1536]{1,0:T(8,128)(2,1)} %all-gather.3.cloned.1.call-done.right_hbm.fr_ref, f32[16,128,128]{2,1,0:T(8,128)S(1)} %convolution_add_fusion.p_ref, f32[16,128]{1,0:T(8,128)S(1)} %broadcast_divide_fusion.d_ref, ...), custom_call_target="tpu_custom_call" | custom-call | tf_op jit(solution)/shard_map/pallas_call | solution.py:96
  188.4 3.1 %collective-permute-start.6 = (bf16[512,128]{0,1:T(8,128)(2,1)S(1)}, bf16[512,128]{0,1:T(8,128)(2,1)S(1)}, u32[]{:S(2)}, u32[]{:S(2)}) collective-permute-start(bf16[512,128]{0,1:T(8,128)(2,1)S(1)} %get-tuple-element.16), channel_id=1, source_target_pairs={{64,0},{65,1},{66,2},{67,3},{68,4},{69,5},{70,6},{71,7},{72,8},{73... | collective-permute-start | bytes 393224 | tf_op jit(solution)/shard_map/ppermute | solution.py:109
  191.5 1.3 collective-permute-start.5
  192.8 1.3 collective-permute-start.4
  194.1 1.3 collective-permute-start.3
  195.4 1.3 collective-permute-done.4
  196.7 1.4 collective-permute-done.3
  198.2 9.8 %all-gather.5.cloned.1.call-done = bf16[2048,1024]{1,0:T(8,128)(2,1)} async-done(((bf16[256,1024]{1,0:T(8,128)(2,1)}), bf16[2048,1024]{1,0:T(8,128)(2,1)}) %all-gather.5.cloned.1.call-update) | async-done | bytes 4194320 | tf_op jit(solution)/shard_map/all_gather | solution.py:166
  208.0 1.3 collective-permute-start.7
  209.3 3.0 %fusion.76 = f32[1024,128]{0,1:T(8,128)S(1)} fusion(bf16[2048,128]{0,1:T(8,128)(2,1)S(1)} %broadcast_select_fusion, bf16[2048,1024]{1,0:T(8,128)(2,1)} %all-gather.5.cloned.1.call-done), kind=kOutput, calls=%fused_computation.148 | convolution fusion | flops 536870912 | bytes 5242880 | tf_op jit(solution)/shard_map/dot_general | solution.py:187
  212.4 5.0 %collective-permute-done.7 = bf16[2048,1024]{1,0:T(8,128)(2,1)} collective-permute-done((bf16[2048,1024]{1,0:T(8,128)(2,1)}, bf16[2048,1024]{1,0:T(8,128)(2,1)}, u32[]{:S(2)}, u32[]{:S(2)}) %collective-permute-start.7) | collective-permute-done | bytes 4194336 | tf_op jit(solution)/shard_map/ppermute | solution.py:180
  217.4 2.9 %fusion.75 = f32[1024,128]{0,1:T(8,128)S(1)} fusion(bf16[2048,128]{0,1:T(8,128)(2,1)S(1)} %broadcast_select_fusion, bf16[2048,1024]{1,0:T(8,128)(2,1)} %collective-permute-done.7), kind=kOutput, calls=%fused_computation.147 | convolution fusion | flops 536870912 | bytes 5242880 | tf_op jit(solution)/shard_map/dot_general | solution.py:186
  220.5 1.3 collective-permute-start.8
  221.8 2.5 collective-permute-done.8
  224.5 14.4 %shard_map.75 = bf16[128,2048]{1,0:T(8,128)(2,1)S(1)} custom-call(bf16[2048,1536]{1,0:T(8,128)(2,1)} %collective-permute-done.1.left_hbm.fl_ref, bf16[2048,1536]{1,0:T(8,128)(2,1)} %all-gather.3.cloned.1.call-done.right_hbm.fr_ref, f32[16,128,128]{2,1,0:T(8,128)S(1)} %convolution_add_fusion.p_ref, f32[16,128]{1,0:T(8,128)S(1)} %broadcast_divide_fusion.d_ref, ...), custom_call_target="tpu_custom_call" | custom-call | tf_op jit(solution)/shard_map/pallas_call | solution.py:96
  239.0 1.3 collective-permute-start.12
  240.3 1.3 collective-permute-start.11
  241.6 1.3 collective-permute-start.10
  242.9 1.3 collective-permute-start.9
  244.2 3.1 %collective-permute-done.12 = bf16[512,128]{0,1:T(8,128)(2,1)S(1)} collective-permute-done((bf16[512,128]{0,1:T(8,128)(2,1)S(1)}, bf16[512,128]{0,1:T(8,128)(2,1)S(1)}, u32[]{:S(2)}, u32[]{:S(2)}) %collective-permute-start.12) | collective-permute-done | bytes 131104 | tf_op jit(solution)/shard_map/ppermute | solution.py:109
  247.3 2.8 %collective-permute-done.11 = bf16[512,128]{0,1:T(8,128)(2,1)S(1)} collective-permute-done((bf16[512,128]{0,1:T(8,128)(2,1)S(1)}, bf16[512,128]{0,1:T(8,128)(2,1)S(1)}, u32[]{:S(2)}, u32[]{:S(2)}) %collective-permute-start.11) | collective-permute-done | bytes 131104 | tf_op jit(solution)/shard_map/ppermute | solution.py:109
  250.1 2.8 %collective-permute-done.10 = bf16[512,128]{0,1:T(8,128)(2,1)S(1)} collective-permute-done((bf16[512,128]{0,1:T(8,128)(2,1)S(1)}, bf16[512,128]{0,1:T(8,128)(2,1)S(1)}, u32[]{:S(2)}, u32[]{:S(2)}) %collective-permute-start.10) | collective-permute-done | bytes 131104 | tf_op jit(solution)/shard_map/ppermute | solution.py:109
  252.9 2.0 collective-permute-done.9
  255.1 1.0 copy.19
  (83 shorter events, 14.0 us)
Async XLA Ops:
  6.5 109.6 %copy-start = (bf16[512,128]{1,0:T(8,128)(2,1)S(1)}, bf16[512,128]{1,0:T(8,128)(2,1)}, u32[]{:S(2)}) copy-start(bf16[512,128]{1,0:T(8,128)(2,1)} %param.9) | copy-start | bytes 393220
  6.5 114.9 %copy-start.7 = (s32[8]{0:T(128)S(1)}, s32[8]{0:T(128)}, u32[]{:S(2)}) copy-start(s32[8]{0:T(128)} %param.10) | copy-start | bytes 100
  6.5 114.7 %copy-start.6 = (bf16[2048,128]{1,0:T(8,128)(2,1)S(1)}, bf16[2048,128]{1,0:T(8,128)(2,1)}, u32[]{:S(2)}) copy-start(bf16[2048,128]{1,0:T(8,128)(2,1)} %param.13) | copy-start | bytes 1572868
  6.5 101.9 %all-gather.3.cloned.1.call-start = ((), (), s32[]{:S(2)}) async-start(), calls=%async_computation.1 | async-start | bytes 7077888 | tf_op jit(solution)/shard_map/all_gather | solution.py:152
  6.5 1.6 collective-permute-start
  108.5 47.2 %collective-permute-start.1 = (bf16[2048,1536]{1,0:T(8,128)(2,1)}, bf16[2048,1536]{1,0:T(8,128)(2,1)}, u32[]{:S(2)}, u32[]{:S(2)}) collective-permute-start(bf16[2048,1536]{1,0:T(8,128)(2,1)} %all-gather.3.cloned.1.call-done.right_hbm.fr_ref), channel_id=1, source_target_pairs={{128,0},{64,192},{129,1},{65,193},{130,2},{66,194},{131,3},{67,195... | collective-permute-start | bytes 18874376 | tf_op jit(solution)/shard_map/ppermute | solution.py:154
  117.8 6.8 %all-to-all-start = ((bf16[4,128,128]{2,1,0:T(8,128)(2,1)}), bf16[4,128,128]{2,1,0:T(8,128)(2,1)S(1)}, u32[]{:S(2)}, u32[]{:S(2)}) async-start(bf16[4,128,128]{2,1,0:T(8,128)(2,1)} %bitcast.5), calls=%async_computation | async-start | bytes 262144 | tf_op jit(solution)/shard_map/all_to_all | solution.py:132
  121.1 86.8 %all-gather.5.cloned.1.call-start = ((), (), s32[]{:S(2)}) async-start(), calls=%async_computation.2 | async-start | bytes 4718592 | tf_op jit(solution)/shard_map/all_gather | solution.py:166
  121.4 34.0 %copy-start.3 = (bf16[2048,128]{0,1:T(8,128)(2,1)}, bf16[2048,128]{0,1:T(8,128)(2,1)S(1)}, u32[]{:S(2)}) copy-start(bf16[2048,128]{0,1:T(8,128)(2,1)S(1)} %copy.14) | copy-start | bytes 1572868
  132.8 22.7 %collective-permute-start.2 = (bf16[2048,128]{0,1:T(8,128)(2,1)S(1)}, bf16[2048,128]{0,1:T(8,128)(2,1)S(1)}, u32[]{:S(2)}, u32[]{:S(2)}) collective-permute-start(bf16[2048,128]{0,1:T(8,128)(2,1)S(1)} %get-tuple-element.21), channel_id=1, source_target_pairs={{0,128},{1,129},{2,130},{3,131},{4,132},{5,133},{6,134},{7,135},{8... | collective-permute-start | bytes 1572872 | tf_op jit(solution)/shard_map/ppermute | solution.py:174
  157.6 3.5 %copy-start.5 = (bf16[16,128,128]{2,1,0:T(8,128)(2,1)S(1)}, bf16[16,128,128]{2,1,0:T(8,128)(2,1)}, u32[]{:S(2)}) copy-start(bf16[16,128,128]{2,1,0:T(8,128)(2,1)} %shard_map.73) | copy-start | bytes 1572868
  188.4 7.0 %collective-permute-start.6 = (bf16[512,128]{0,1:T(8,128)(2,1)S(1)}, bf16[512,128]{0,1:T(8,128)(2,1)S(1)}, u32[]{:S(2)}, u32[]{:S(2)}) collective-permute-start(bf16[512,128]{0,1:T(8,128)(2,1)S(1)} %get-tuple-element.16), channel_id=1, source_target_pairs={{64,0},{65,1},{66,2},{67,3},{68,4},{69,5},{70,6},{71,7},{72,8},{73... | collective-permute-start | bytes 393224 | tf_op jit(solution)/shard_map/ppermute | solution.py:109
  191.5 3.9 %collective-permute-start.5 = (bf16[512,128]{0,1:T(8,128)(2,1)S(1)}, bf16[512,128]{0,1:T(8,128)(2,1)S(1)}, u32[]{:S(2)}, u32[]{:S(2)}) collective-permute-start(bf16[512,128]{0,1:T(8,128)(2,1)S(1)} %get-tuple-element.17), channel_id=1, source_target_pairs={{64,0},{65,1},{66,2},{67,3},{68,4},{69,5},{70,6},{71,7},{72,8},{73... | collective-permute-start | bytes 393224 | tf_op jit(solution)/shard_map/ppermute | solution.py:109
  192.8 4.0 %collective-permute-start.4 = (bf16[512,128]{0,1:T(8,128)(2,1)S(1)}, bf16[512,128]{0,1:T(8,128)(2,1)S(1)}, u32[]{:S(2)}, u32[]{:S(2)}) collective-permute-start(bf16[512,128]{0,1:T(8,128)(2,1)S(1)} %get-tuple-element.18), channel_id=1, source_target_pairs={{64,0},{65,1},{66,2},{67,3},{68,4},{69,5},{70,6},{71,7},{72,8},{73... | collective-permute-start | bytes 393224 | tf_op jit(solution)/shard_map/ppermute | solution.py:109
  194.1 4.1 %collective-permute-start.3 = (bf16[512,128]{0,1:T(8,128)(2,1)S(1)}, bf16[512,128]{0,1:T(8,128)(2,1)S(1)}, u32[]{:S(2)}, u32[]{:S(2)}) collective-permute-start(bf16[512,128]{0,1:T(8,128)(2,1)S(1)} %get-tuple-element.15), channel_id=1, source_target_pairs={{64,0},{65,1},{66,2},{67,3},{68,4},{69,5},{70,6},{71,7},{72,8},{73... | collective-permute-start | bytes 393224 | tf_op jit(solution)/shard_map/ppermute | solution.py:109
  208.0 9.4 %collective-permute-start.7 = (bf16[2048,1024]{1,0:T(8,128)(2,1)}, bf16[2048,1024]{1,0:T(8,128)(2,1)}, u32[]{:S(2)}, u32[]{:S(2)}) collective-permute-start(bf16[2048,1024]{1,0:T(8,128)(2,1)} %all-gather.5.cloned.1.call-done), channel_id=1, source_target_pairs={{0,128},{192,64},{1,129},{193,65},{2,130},{194,66},{3,131},{195,67... | collective-permute-start | bytes 12582920 | tf_op jit(solution)/shard_map/ppermute | solution.py:180
  209.3 11.0 %copy-start.2 = (f32[2048,128]{0,1:T(8,128)S(1)}, f32[2048,128]{0,1:T(8,128)}, u32[]{:S(2)}) copy-start(f32[2048,128]{0,1:T(8,128)} %get-tuple-element.22) | copy-start | bytes 3145732
  212.4 11.9 %copy-start.4 = (bf16[2048,128]{0,1:T(8,128)(2,1)S(1)}, bf16[2048,128]{0,1:T(8,128)(2,1)}, u32[]{:S(2)}) copy-start(bf16[2048,128]{0,1:T(8,128)(2,1)} %copy-done.3) | copy-start | bytes 1572868
  220.5 3.8 %collective-permute-start.8 = (bf16[2048,128]{0,1:T(8,128)(2,1)S(1)}, bf16[2048,128]{0,1:T(8,128)(2,1)S(1)}, u32[]{:S(2)}, u32[]{:S(2)}) collective-permute-start(bf16[2048,128]{0,1:T(8,128)(2,1)S(1)} %fusion.8), channel_id=1, source_target_pairs={{128,0},{129,1},{130,2},{131,3},{132,4},{133,5},{134,6},{135,7},{1... | collective-permute-start | bytes 1572872 | tf_op jit(solution)/shard_map/ppermute | solution.py:193
  224.5 31.6 %copy-start.1 = (bf16[512,128]{1,0:T(8,128)(2,1)S(1)}, bf16[512,128]{1,0:T(8,128)(2,1)}, u32[]{:S(2)}) copy-start(bf16[512,128]{1,0:T(8,128)(2,1)} %param.9) | copy-start | bytes 393220
  239.0 8.3 %collective-permute-start.12 = (bf16[512,128]{0,1:T(8,128)(2,1)S(1)}, bf16[512,128]{0,1:T(8,128)(2,1)S(1)}, u32[]{:S(2)}, u32[]{:S(2)}) collective-permute-start(bf16[512,128]{0,1:T(8,128)(2,1)S(1)} %get-tuple-element.12), channel_id=1, source_target_pairs={{0,64},{1,65},{2,66},{3,67},{4,68},{5,69},{6,70},{7,71},{8,72},{9,... | collective-permute-start | bytes 393224 | tf_op jit(solution)/shard_map/ppermute | solution.py:109
  240.3 9.8 %collective-permute-start.11 = (bf16[512,128]{0,1:T(8,128)(2,1)S(1)}, bf16[512,128]{0,1:T(8,128)(2,1)S(1)}, u32[]{:S(2)}, u32[]{:S(2)}) collective-permute-start(bf16[512,128]{0,1:T(8,128)(2,1)S(1)} %get-tuple-element.13), channel_id=1, source_target_pairs={{0,64},{1,65},{2,66},{3,67},{4,68},{5,69},{6,70},{7,71},{8,72},{9,... | collective-permute-start | bytes 393224 | tf_op jit(solution)/shard_map/ppermute | solution.py:109
  241.6 11.3 %collective-permute-start.10 = (bf16[512,128]{0,1:T(8,128)(2,1)S(1)}, bf16[512,128]{0,1:T(8,128)(2,1)S(1)}, u32[]{:S(2)}, u32[]{:S(2)}) collective-permute-start(bf16[512,128]{0,1:T(8,128)(2,1)S(1)} %get-tuple-element.14), channel_id=1, source_target_pairs={{0,64},{1,65},{2,66},{3,67},{4,68},{5,69},{6,70},{7,71},{8,72},{9,... | collective-permute-start | bytes 393224 | tf_op jit(solution)/shard_map/ppermute | solution.py:109
  242.9 12.0 %collective-permute-start.9 = (bf16[512,128]{0,1:T(8,128)(2,1)S(1)}, bf16[512,128]{0,1:T(8,128)(2,1)S(1)}, u32[]{:S(2)}, u32[]{:S(2)}) collective-permute-start(bf16[512,128]{0,1:T(8,128)(2,1)S(1)} %get-tuple-element.11), channel_id=1, source_target_pairs={{0,64},{1,65},{2,66},{3,67},{4,68},{5,69},{6,70},{7,71},{8,72},{9,... | collective-permute-start | bytes 393224 | tf_op jit(solution)/shard_map/ppermute | solution.py:109
Sparse Core Ops, SparseCore 0:
  30.8 77.6 all-gather.2
  155.6 52.3 all-gather.4

commit v2 on v1

--- a/solution.py
+++ b/solution.py
@@ -102,11 +102,6 @@
         compiler_params=pltpu.CompilerParams(vmem_limit_bytes=48 * 1024 * 1024),
     )(left, right, prod, inv_diag, rhs.T)
     return out_t.T
-
-
-def chunked_permute(x, axis, perm, parts=4):
-    pieces = jnp.split(x, parts, axis=0)
-    return jnp.concatenate([lax.ppermute(p, axis, perm) for p in pieces], axis=0)
 
 
 def ancestor_values(solved, owners, indices, counts):
@@ -174,7 +169,7 @@
     other_one = lax.ppermute(own_one, "row", [(0, 1)])
     reduced_one = rhs_values - own_one.astype(jnp.float32) - other_one.astype(jnp.float32)
     sol_one = kernel_solve(crit_left, crit_right, prod, inv_diag, reduced_one)
-    got_one = chunked_permute(sol_one, "col", left)
+    got_one = lax.ppermute(sol_one, "col", left)
     half_two, got_one = lax.optimization_barrier((half_two, got_one))
     sol_one = jnp.where(col_index == 1, sol_one, got_one)
     prod_left = lax.ppermute(half_two, ("row", "col"), [(0, 2), (3, 1)])
@@ -193,7 +188,7 @@
     other_zero = lax.ppermute(own_zero, "row", down)
     reduced_zero = rhs_values - own_zero.astype(jnp.float32) - other_zero.astype(jnp.float32)
     sol_zero = kernel_solve(crit_left, crit_right, prod, inv_diag, reduced_zero)
-    got_zero = chunked_permute(sol_zero, "col", right)
+    got_zero = lax.ppermute(sol_zero, "col", right)
     sol_zero = jnp.where(col_index == 0, sol_zero, got_zero)
     return jnp.where(row_index == 1, sol_one, sol_zero)
 

time: 264 us -> 264 us (level)
  waiting for transfers between devices: 112 us -> 120 us
  starting transfers between devices: 23.7 us -> 16 us
    ppermute x8 -> x2, waiting for transfers between devices: 13.4 us -> 21.2 us  [the longest x1 14.6 us: device_body(): got_zero = lax.ppermute(sol_zero, 'col', right)]
    ppermute x8 -> x2, starting transfers between devices: 12.1 us -> 4.41 us  [the longest x1 3.11 us: device_body(): got_one = lax.ppermute(sol_one, 'col', left)]
  transfers between devices with their start and end apart: 16 -> 10, of which waited for: 12 -> 8; matrix products, arithmetic and copies ran while one was open for 13% -> 13% of each run, Pallas kernels for 6% -> 6%
where the time goes in v2:
time: 264 us; the launch traced here: 263 us
  waiting for transfers between devices  120 us (45%)
  blocking collectives  42.7 us (16%)
  Pallas kernels  30.8 us (12%)
  matrix products  21.8 us (8%)
  starting transfers between devices  16 us (6%)
  between operations  14 us (5%)
  local copies, waits for them, and re-layouts  13 us (5%)
  other arithmetic  4.22 us (2%)
    all_gather x1, waiting for transfers between devices, device_body(): both = lax.all_gather(both, 'z', axis=0, tiled=True)  77.8 us
    pallas_call x2, Pallas kernels, kernel_solve(): pl.pallas_call(solve_kernel, out_shape=jax.ShapeDtypeStruct((cols, n), jn...  28.9 us
    all_gather x1, blocking collectives, device_body(): half_two = lax.all_gather(half_two, 'y', axis=0, tiled=True)  14.7 us
    ppermute x1, waiting for transfers between devices, device_body(): got_zero = lax.ppermute(sol_zero, 'col', right)  14.6 us
    all_gather x1, blocking collectives, device_body(): both = lax.all_gather(both, 'y', axis=0, tiled=True)  14.6 us
    all_gather x1, waiting for transfers between devices, device_body(): half_two = lax.all_gather(half_two, 'z', axis=0, tiled=True)  9.94 us
    all_gather x1, blocking collectives, device_body(): both = lax.all_gather(both, 'xh', axis=0, tiled=True)  7.02 us
    ppermute x1, waiting for transfers between devices, device_body(): got_one = lax.ppermute(sol_one, 'col', left)  6.65 us
  transfers between devices with their start and end apart: 10, of which 8 were waited for; matrix products, arithmetic and copies ran while one was open for 13% of the time, Pallas kernels for 6%

profile of v2, /device:TPU:6, one launch (start us, length us, event | category | flops | bytes accessed | tf_op | source)
XLA Modules:
  0.0 262.7 jit_solution(11272049269986487240)
XLA Ops:
  6.7 0.9 reshape.122
  7.5 0.7 collective-permute-done
  8.2 0.9 broadcast_select_fusion.3
  9.1 7.0 %all_gather.18 = bf16[64,1536]{1,0:T(8,128)(2,1)S(1)} all-gather(bf16[32,1536]{1,0:T(8,128)(2,1)S(1)} %pad_maximum_fusion), channel_id=1, replica_groups=mesh['row'=2,'col'=2,'z'=8,'y'=4,'xh'=2] {'xh'}, dimensions={0}, use_global_device_ids=true | all-gather | bytes 294912 | tf_op jit(solution)/shard_map/all_gather | solution.py:144
  16.1 14.6 %all_gather.19 = bf16[256,1536]{1,0:T(8,128)(2,1)} all-gather(bf16[64,1536]{1,0:T(8,128)(2,1)S(1)} %all_gather.18), channel_id=1, replica_groups=mesh['row'=2,'col'=2,'z'=8,'y'=4,'xh'=2] {'y'}, dimensions={0}, use_global_device_ids=true | all-gather | bytes 983040 | tf_op jit(solution)/shard_map/all_gather | solution.py:145
  30.7 77.8 %all-gather.3.cloned.1.call-done.right_hbm.fr_ref = bf16[2048,1536]{1,0:T(8,128)(2,1)} async-done(((bf16[256,1536]{1,0:T(8,128)(2,1)}), bf16[2048,1536]{1,0:T(8,128)(2,1)}) %all-gather.3.cloned.1.call-update) | async-done | bytes 6291472 | tf_op jit(solution)/shard_map/all_gather | solution.py:147
  108.5 4.2 %collective-permute-start.1 = (bf16[2048,1536]{1,0:T(8,128)(2,1)}, bf16[2048,1536]{1,0:T(8,128)(2,1)}, u32[]{:S(2)}, u32[]{:S(2)}) collective-permute-start(bf16[2048,1536]{1,0:T(8,128)(2,1)} %all-gather.3.cloned.1.call-done.right_hbm.fr_ref), channel_id=1, source_target_pairs={{128,0},{64,192},{129,1},{65,193},{130,2},{66,194},{131,3},{67,195... | collective-permute-start | bytes 18874376 | tf_op jit(solution)/shard_map/ppermute | solution.py:149
  112.7 0.7 broadcast_compare_fusion
  113.5 1.2 gather_fusion.1
  114.8 1.3 gather_fusion
  116.1 0.9 gather_fusion.2
  117.2 0.7 broadcast_in_dim.28
  117.8 3.3 %all-to-all-start = ((bf16[4,128,128]{2,1,0:T(8,128)(2,1)}), bf16[4,128,128]{2,1,0:T(8,128)(2,1)S(1)}, u32[]{:S(2)}, u32[]{:S(2)}) async-start(bf16[4,128,128]{2,1,0:T(8,128)(2,1)} %bitcast.5), calls=%async_computation | async-start | bytes 262144 | tf_op jit(solution)/shard_map/all_to_all | solution.py:127
  121.5 3.0 %all-to-all-done = bf16[4,128,128]{2,1,0:T(8,128)(2,1)S(1)} async-done(((bf16[4,128,128]{2,1,0:T(8,128)(2,1)}), bf16[4,128,128]{2,1,0:T(8,128)(2,1)S(1)}, u32[]{:S(2)}, u32[]{:S(2)}) %all-to-all-start) | async-done | bytes 131104 | tf_op jit(solution)/shard_map/all_to_all | solution.py:127
  124.6 0.6 gather_fusion.3
  125.2 3.1 %slice.23 = bf16[2048,512]{1,0:T(8,128)(2,1)} slice(bf16[2048,1536]{1,0:T(8,128)(2,1)} %all-gather.3.cloned.1.call-done.right_hbm.fr_ref), slice={[0:2048], [1024:1536]} | slice | bytes 4194304 | tf_op jit(solution)/shard_map/slice | solution.py:148
  128.2 3.1 %reshape_reshape.3 = bf16[512,2048]{1,0:T(8,128)(2,1)S(1)} reshape(bf16[2048,512]{1,0:T(8,128)(2,1)} %slice.23) | data formatting | bytes 4194304 | tf_op jit(solution)/shard_map/reshape;reshape | solution.py:148
  131.3 1.5 fusion.71
  132.8 1.4 collective-permute-start.2
  134.3 6.4 %all_gather.21 = bf16[64,1024]{1,0:T(8,128)(2,1)S(1)} all-gather(bf16[32,1024]{1,0:T(8,128)(2,1)S(1)} %get-tuple-element.12), channel_id=1, replica_groups=mesh['row'=2,'col'=2,'z'=8,'y'=4,'xh'=2] {'xh'}, dimensions={0}, use_global_device_ids=true | all-gather | bytes 196608 | tf_op jit(solution)/shard_map/all_gather | solution.py:158
  140.8 14.7 %all_gather.22 = bf16[256,1024]{1,0:T(8,128)(2,1)} all-gather(bf16[64,1024]{1,0:T(8,128)(2,1)S(1)} %all_gather.21), channel_id=1, replica_groups=mesh['row'=2,'col'=2,'z'=8,'y'=4,'xh'=2] {'y'}, dimensions={0}, use_global_device_ids=true | all-gather | bytes 655360 | tf_op jit(solution)/shard_map/all_gather | solution.py:159
  155.7 1.9 shard_map.73
  157.7 1.4 fusion.1
  159.1 2.0 fusion.17
  161.2 0.9 convolution_add_fusion.23
  162.0 0.9 convolution_add_fusion.22
  166.8 0.5 fusion.39
  167.3 0.5 convolution_add_fusion.21
  167.8 0.5 convolution_add_fusion.20
  168.9 0.3 convolution_add_fusion.16
  169.9 0.3 convolution_add_fusion.12
  170.8 0.3 convolution_add_fusion.8
  172.0 0.3 convolution_add_fusion.5
  173.3 0.5 convolution_add_fusion.p_ref
  173.8 14.5 %shard_map.74 = bf16[128,2048]{1,0:T(8,128)(2,1)S(1)} custom-call(bf16[2048,1536]{1,0:T(8,128)(2,1)} %collective-permute-done.1.left_hbm.fl_ref, bf16[2048,1536]{1,0:T(8,128)(2,1)} %all-gather.3.cloned.1.call-done.right_hbm.fr_ref, f32[16,128,128]{2,1,0:T(8,128)S(1)} %convolution_add_fusion.p_ref, f32[16,128]{1,0:T(8,128)S(1)} %broadcast_divide_fusion.d_ref, ...), custom_call_target="tpu_custom_call" | custom-call | tf_op jit(solution)/shard_map/pallas_call | solution.py:96
  188.3 3.1 %collective-permute-start.3 = (bf16[2048,128]{0,1:T(8,128)(2,1)S(1)}, bf16[2048,128]{0,1:T(8,128)(2,1)S(1)}, u32[]{:S(2)}, u32[]{:S(2)}) collective-permute-start(bf16[2048,128]{0,1:T(8,128)(2,1)S(1)} %bitcast.25), channel_id=1, source_target_pairs={{64,0},{65,1},{66,2},{67,3},{68,4},{69,5},{70,6},{71,7},{72,8},{73... | collective-permute-start | bytes 1572872 | tf_op jit(solution)/shard_map/ppermute | solution.py:172
  191.4 6.6 %collective-permute-done.3 = bf16[2048,128]{0,1:T(8,128)(2,1)S(1)} collective-permute-done((bf16[2048,128]{0,1:T(8,128)(2,1)S(1)}, bf16[2048,128]{0,1:T(8,128)(2,1)S(1)}, u32[]{:S(2)}, u32[]{:S(2)}) %collective-permute-start.3) | collective-permute-done | bytes 524320 | tf_op jit(solution)/shard_map/ppermute | solution.py:172
  198.1 9.9 %all-gather.5.cloned.1.call-done = bf16[2048,1024]{1,0:T(8,128)(2,1)} async-done(((bf16[256,1024]{1,0:T(8,128)(2,1)}), bf16[2048,1024]{1,0:T(8,128)(2,1)}) %all-gather.5.cloned.1.call-update) | async-done | bytes 4194320 | tf_op jit(solution)/shard_map/all_gather | solution.py:161
  208.0 1.3 collective-permute-start.4
  209.4 3.0 %fusion.73 = f32[1024,128]{0,1:T(8,128)S(1)} fusion(bf16[2048,128]{0,1:T(8,128)(2,1)S(1)} %broadcast_select_fusion, bf16[2048,1024]{1,0:T(8,128)(2,1)} %all-gather.5.cloned.1.call-done), kind=kOutput, calls=%fused_computation.144 | convolution fusion | flops 536870912 | bytes 5242880 | tf_op jit(solution)/shard_map/dot_general | solution.py:182
  212.4 5.0 %collective-permute-done.4 = bf16[2048,1024]{1,0:T(8,128)(2,1)} collective-permute-done((bf16[2048,1024]{1,0:T(8,128)(2,1)}, bf16[2048,1024]{1,0:T(8,128)(2,1)}, u32[]{:S(2)}, u32[]{:S(2)}) %collective-permute-start.4) | collective-permute-done | bytes 4194336 | tf_op jit(solution)/shard_map/ppermute | solution.py:175
  217.4 2.9 %fusion.72 = f32[1024,128]{0,1:T(8,128)S(1)} fusion(bf16[2048,128]{0,1:T(8,128)(2,1)S(1)} %broadcast_select_fusion, bf16[2048,1024]{1,0:T(8,128)(2,1)} %collective-permute-done.4), kind=kOutput, calls=%fused_computation.143 | convolution fusion | flops 536870912 | bytes 5242880 | tf_op jit(solution)/shard_map/dot_general | solution.py:181
  220.5 1.3 collective-permute-start.5
  221.8 2.5 collective-permute-done.5
  224.5 14.4 %shard_map.75 = bf16[128,2048]{1,0:T(8,128)(2,1)S(1)} custom-call(bf16[2048,1536]{1,0:T(8,128)(2,1)} %collective-permute-done.1.left_hbm.fl_ref, bf16[2048,1536]{1,0:T(8,128)(2,1)} %all-gather.3.cloned.1.call-done.right_hbm.fr_ref, f32[16,128,128]{2,1,0:T(8,128)S(1)} %convolution_add_fusion.p_ref, f32[16,128]{1,0:T(8,128)S(1)} %broadcast_divide_fusion.d_ref, ...), custom_call_target="tpu_custom_call" | custom-call | tf_op jit(solution)/shard_map/pallas_call | solution.py:96
  238.9 1.3 collective-permute-start.6
  240.2 14.6 %collective-permute-done.6 = bf16[2048,128]{0,1:T(8,128)(2,1)S(1)} collective-permute-done((bf16[2048,128]{0,1:T(8,128)(2,1)S(1)}, bf16[2048,128]{0,1:T(8,128)(2,1)S(1)}, u32[]{:S(2)}, u32[]{:S(2)}) %collective-permute-start.6) | collective-permute-done | bytes 524320 | tf_op jit(solution)/shard_map/ppermute | solution.py:191
  254.9 1.0 copy.19
  (68 shorter events, 9.2 us)
Async XLA Ops:
  6.5 109.6 %copy-start = (bf16[512,128]{1,0:T(8,128)(2,1)S(1)}, bf16[512,128]{1,0:T(8,128)(2,1)}, u32[]{:S(2)}) copy-start(bf16[512,128]{1,0:T(8,128)(2,1)} %param.9) | copy-start | bytes 393220
  6.5 114.9 %copy-start.7 = (s32[8]{0:T(128)S(1)}, s32[8]{0:T(128)}, u32[]{:S(2)}) copy-start(s32[8]{0:T(128)} %param.10) | copy-start | bytes 100
  6.5 114.7 %copy-start.6 = (bf16[2048,128]{1,0:T(8,128)(2,1)S(1)}, bf16[2048,128]{1,0:T(8,128)(2,1)}, u32[]{:S(2)}) copy-start(bf16[2048,128]{1,0:T(8,128)(2,1)} %param.13) | copy-start | bytes 1572868
  6.5 101.9 %all-gather.3.cloned.1.call-start = ((), (), s32[]{:S(2)}) async-start(), calls=%async_computation.1 | async-start | bytes 7077888 | tf_op jit(solution)/shard_map/all_gather | solution.py:147
  6.5 1.6 collective-permute-start
  108.5 47.2 %collective-permute-start.1 = (bf16[2048,1536]{1,0:T(8,128)(2,1)}, bf16[2048,1536]{1,0:T(8,128)(2,1)}, u32[]{:S(2)}, u32[]{:S(2)}) collective-permute-start(bf16[2048,1536]{1,0:T(8,128)(2,1)} %all-gather.3.cloned.1.call-done.right_hbm.fr_ref), channel_id=1, source_target_pairs={{128,0},{64,192},{129,1},{65,193},{130,2},{66,194},{131,3},{67,195... | collective-permute-start | bytes 18874376 | tf_op jit(solution)/shard_map/ppermute | solution.py:149
  117.8 6.8 %all-to-all-start = ((bf16[4,128,128]{2,1,0:T(8,128)(2,1)}), bf16[4,128,128]{2,1,0:T(8,128)(2,1)S(1)}, u32[]{:S(2)}, u32[]{:S(2)}) async-start(bf16[4,128,128]{2,1,0:T(8,128)(2,1)} %bitcast.5), calls=%async_computation | async-start | bytes 262144 | tf_op jit(solution)/shard_map/all_to_all | solution.py:127
  121.2 86.8 %all-gather.5.cloned.1.call-start = ((), (), s32[]{:S(2)}) async-start(), calls=%async_computation.2 | async-start | bytes 4718592 | tf_op jit(solution)/shard_map/all_gather | solution.py:161
  121.4 34.0 %copy-start.3 = (bf16[2048,128]{0,1:T(8,128)(2,1)}, bf16[2048,128]{0,1:T(8,128)(2,1)S(1)}, u32[]{:S(2)}) copy-start(bf16[2048,128]{0,1:T(8,128)(2,1)S(1)} %copy.14) | copy-start | bytes 1572868
  132.8 22.7 %collective-permute-start.2 = (bf16[2048,128]{0,1:T(8,128)(2,1)S(1)}, bf16[2048,128]{0,1:T(8,128)(2,1)S(1)}, u32[]{:S(2)}, u32[]{:S(2)}) collective-permute-start(bf16[2048,128]{0,1:T(8,128)(2,1)S(1)} %get-tuple-element.13), channel_id=1, source_target_pairs={{0,128},{1,129},{2,130},{3,131},{4,132},{5,133},{6,134},{7,135},{8... | collective-permute-start | bytes 1572872 | tf_op jit(solution)/shard_map/ppermute | solution.py:169
  157.7 3.5 %copy-start.5 = (bf16[16,128,128]{2,1,0:T(8,128)(2,1)S(1)}, bf16[16,128,128]{2,1,0:T(8,128)(2,1)}, u32[]{:S(2)}) copy-start(bf16[16,128,128]{2,1,0:T(8,128)(2,1)} %shard_map.73) | copy-start | bytes 1572868
  188.3 9.8 %collective-permute-start.3 = (bf16[2048,128]{0,1:T(8,128)(2,1)S(1)}, bf16[2048,128]{0,1:T(8,128)(2,1)S(1)}, u32[]{:S(2)}, u32[]{:S(2)}) collective-permute-start(bf16[2048,128]{0,1:T(8,128)(2,1)S(1)} %bitcast.25), channel_id=1, source_target_pairs={{64,0},{65,1},{66,2},{67,3},{68,4},{69,5},{70,6},{71,7},{72,8},{73... | collective-permute-start | bytes 1572872 | tf_op jit(solution)/shard_map/ppermute | solution.py:172
  208.0 9.4 %collective-permute-start.4 = (bf16[2048,1024]{1,0:T(8,128)(2,1)}, bf16[2048,1024]{1,0:T(8,128)(2,1)}, u32[]{:S(2)}, u32[]{:S(2)}) collective-permute-start(bf16[2048,1024]{1,0:T(8,128)(2,1)} %all-gather.5.cloned.1.call-done), channel_id=1, source_target_pairs={{0,128},{192,64},{1,129},{193,65},{2,130},{194,66},{3,131},{195,67... | collective-permute-start | bytes 12582920 | tf_op jit(solution)/shard_map/ppermute | solution.py:175
  209.4 10.9 %copy-start.2 = (f32[2048,128]{0,1:T(8,128)S(1)}, f32[2048,128]{0,1:T(8,128)}, u32[]{:S(2)}) copy-start(f32[2048,128]{0,1:T(8,128)} %get-tuple-element.14) | copy-start | bytes 3145732
  212.4 11.9 %copy-start.4 = (bf16[2048,128]{0,1:T(8,128)(2,1)S(1)}, bf16[2048,128]{0,1:T(8,128)(2,1)}, u32[]{:S(2)}) copy-start(bf16[2048,128]{0,1:T(8,128)(2,1)} %copy-done.3) | copy-start | bytes 1572868
  220.5 3.8 %collective-permute-start.5 = (bf16[2048,128]{0,1:T(8,128)(2,1)S(1)}, bf16[2048,128]{0,1:T(8,128)(2,1)S(1)}, u32[]{:S(2)}, u32[]{:S(2)}) collective-permute-start(bf16[2048,128]{0,1:T(8,128)(2,1)S(1)} %fusion.8), channel_id=1, source_target_pairs={{128,0},{129,1},{130,2},{131,3},{132,4},{133,5},{134,6},{135,7},{1... | collective-permute-start | bytes 1572872 | tf_op jit(solution)/shard_map/ppermute | solution.py:188
  224.5 31.4 %copy-start.1 = (bf16[512,128]{1,0:T(8,128)(2,1)S(1)}, bf16[512,128]{1,0:T(8,128)(2,1)}, u32[]{:S(2)}) copy-start(bf16[512,128]{1,0:T(8,128)(2,1)} %param.9) | copy-start | bytes 393220
  238.9 15.9 %collective-permute-start.6 = (bf16[2048,128]{0,1:T(8,128)(2,1)S(1)}, bf16[2048,128]{0,1:T(8,128)(2,1)S(1)}, u32[]{:S(2)}, u32[]{:S(2)}) collective-permute-start(bf16[2048,128]{0,1:T(8,128)(2,1)S(1)} %bitcast.26), channel_id=1, source_target_pairs={{0,64},{1,65},{2,66},{3,67},{4,68},{5,69},{6,70},{7,71},{8,72},{9,... | collective-permute-start | bytes 1572872 | tf_op jit(solution)/shard_map/ppermute | solution.py:191
Sparse Core Ops, SparseCore 0:
  30.8 77.6 all-gather.2
  155.6 52.3 all-gather.4
